TPU v7x, 32 devices: a whole 2x2x4 slice. The times are simulated.
32 devices in a mesh: req: 8 (over y, x, core), exp: 4 (over z).
Axes of the slice: x: 2, y: 2, z: 4, core: 2. Of those that a mesh axis runs over, the one named last changes fastest.
Arguments:
- tokens: bfloat16 [4096, 1024], P(('req', 'exp'))
- norm_attn: bfloat16 [1024], replicated, may hold values from 0.099609375 to 1.8984375
- w_query: bfloat16 [1024, 1024], replicated
- w_key: bfloat16 [1024, 512], replicated
- w_value: bfloat16 [1024, 512], replicated, may hold values from -0.1875 to 0.1875
- w_out: bfloat16 [1024, 1024], P('exp'), may hold values from -0.1875 to 0.1875
- norm_moe: bfloat16 [1024], replicated, may hold values from 0.099609375 to 1.8984375
- w_router: bfloat16 [1024, 32], replicated
- w_gate: bfloat16 [32, 1024, 512], P('exp'), may hold values from -0.1875 to 0.1875
- w_up: bfloat16 [32, 1024, 512], P('exp'), may hold values from -0.1875 to 0.1875
- w_down: bfloat16 [32, 512, 1024], P('exp')
- segment_ids: int32 [8, 512], P('req'), may hold values from 0 to 3, never falling along the last dimension, each value on 1 to 256 neighbouring positions
- page_order: int32 [8, 512], P('req'), may hold values from 0 to 511, each once within a row
- expert_ids: int32 [4096, 8], P(('req', 'exp')), may hold values from 0 to 31, all different within a row; in each aligned block of 128 rows (0 to 127, 128 to 255, ...) at most 64 rows name the same one
Outputs:
- mixed: bfloat16 [4096, 1024], P(('req', 'exp'))
- kv_cache: bfloat16 [4096, 8, 128], P('req', 'exp')
Inputs may be any that keep to these rules, and one draw needn't show every extreme that they name: `segment_ids`: along each row, request numbers never fall; every pack holds 4 requests of 1 to 256 positions, one of exactly 256. `page_order`: each row is a permutation of the pack's 512 positions. `expert_ids`: A token's 8 experts differ. Within the rows of one device no expert is named by more than 64 rows, and in some device's rows an expert is named by exactly 64.
All inputs are finite; a program needn't handle non-finite values.
Results may differ from a plain program's by a relative error of at most 0.0055.
Values may be sent and summed in bfloat16 or wider, within the bound.
No kernel may reach another device: no remote copies, remote signals or barrier semaphores. Data moves between devices by JAX's collectives and lax.ppermute only.
A program may use at most 128 MiB of HBM per device.

v0:
```python
import jax
import jax.numpy as jnp
from jax import lax
from jax.sharding import PartitionSpec as P

HD = 64
CAP = 64


def rms_scale(rows, gain):
    rows = rows.astype(jnp.float32)
    inverse = lax.rsqrt(jnp.mean(rows * rows, axis=-1, keepdims=True) + 1e-06)
    return (rows * inverse * gain.astype(jnp.float32)).astype(jnp.bfloat16)


def positions(seg):
    index = jnp.arange(seg.shape[0], dtype=jnp.int32)
    starts = jnp.concatenate([jnp.ones((1,), dtype=bool), seg[1:] != seg[:-1]])
    first = lax.cummax(jnp.where(starts, index, 0), axis=0)
    return index - first


def rotate(values, pos):
    half = values.shape[-1] // 2
    freq = 10000.0 ** (-jnp.arange(half, dtype=jnp.float32) / half)
    angle = pos.astype(jnp.float32)[:, None] * freq[None, :]
    cosine = jnp.cos(angle)[:, None, :]
    sine = jnp.sin(angle)[:, None, :]
    front = values[..., :half]
    back = values[..., half:]
    return jnp.concatenate([front * cosine - back * sine, back * cosine + front * sine], axis=-1)


def attend(query, keyval, seg):
    plen, groups, width = query.shape
    half = width // 2
    block = min(512, plen)
    blocks = plen // block
    queries = query.reshape(blocks, block, groups, 2, half)
    keys = keyval[..., :half]
    values = keyval[..., half:]
    key_pos = jnp.arange(plen, dtype=jnp.int32)
    query_pos = key_pos.reshape(blocks, block)
    query_seg = seg.reshape(blocks, block)

    def one_block(args):
        qblock, qpos, qseg = args
        score = (
            jnp.einsum("qkgd,tkd->kgqt", qblock, keys, preferred_element_type=jnp.float32) * 0.125
        )
        allowed = (qseg[:, None] == seg[None, :]) & (key_pos[None, :] <= qpos[:, None])
        score = jnp.where(allowed[None, None], score, -1e30)
        top = jnp.max(score, axis=-1, keepdims=True)
        expo = jnp.exp(score - top)
        probs = (expo / jnp.sum(expo, axis=-1, keepdims=True)).astype(jnp.bfloat16)
        out = jnp.einsum("kgqt,tkd->qkgd", probs, values, preferred_element_type=jnp.float32)
        return out.astype(jnp.bfloat16)

    outs = lax.map(one_block, (queries, query_pos, query_seg))
    return outs.reshape(plen, groups * width)


def expert_mix(rows_all, ids_all, w_router, w_gate, w_up, w_down):
    tokens_all = rows_all.shape[0]
    local = w_gate.shape[0]
    cap = CAP * lax.axis_size("exp")
    here = lax.axis_index("exp")
    logits = jnp.dot(rows_all, w_router, preferred_element_type=jnp.float32)
    weights = jax.nn.softmax(jnp.take_along_axis(logits, ids_all, axis=1), axis=-1)
    match = (ids_all - here * local)[:, :, None] == jnp.arange(local, dtype=jnp.int32)
    hits = jnp.any(match, axis=1)
    mine = jnp.sum(jnp.where(match, weights[:, :, None], 0.0), axis=1)
    order = jnp.arange(tokens_all, dtype=jnp.int32)
    before = (order[None, :] < order[:, None]).astype(jnp.bfloat16)
    slot = jnp.dot(before, hits.astype(jnp.bfloat16), preferred_element_type=jnp.float32)
    slot = slot.astype(jnp.int32)
    picks = hits.T[:, None, :] & (
        slot.T[:, None, :] == jnp.arange(cap, dtype=jnp.int32)[None, :, None]
    )
    received = jnp.einsum(
        "est,td->esd", picks.astype(jnp.bfloat16), rows_all, preferred_element_type=jnp.float32
    ).astype(jnp.bfloat16)
    gate = jnp.einsum("esd,edf->esf", received, w_gate, preferred_element_type=jnp.float32)
    upward = jnp.einsum("esd,edf->esf", received, w_up, preferred_element_type=jnp.float32)
    hidden = (jax.nn.silu(gate) * upward).astype(jnp.bfloat16)
    result = jnp.einsum("esf,efd->esd", hidden, w_down, preferred_element_type=jnp.float32)
    result = result.astype(jnp.bfloat16)
    combine = jnp.where(picks, mine.T[:, None, :], 0.0)
    high = combine.astype(jnp.bfloat16)
    low = (combine - high.astype(jnp.float32)).astype(jnp.bfloat16)
    partial = jnp.einsum("est,esd->td", high, result, preferred_element_type=jnp.float32)
    partial = partial + jnp.einsum("est,esd->td", low, result, preferred_element_type=jnp.float32)
    return partial


def shards(
    tokens,
    norm_attn,
    w_query,
    w_key,
    w_value,
    w_out,
    norm_moe,
    w_router,
    w_gate,
    w_up,
    w_down,
    segment_ids,
    page_order,
    expert_ids,
):
    rows, width = tokens.shape
    seg = segment_ids[0]
    groups = w_key.shape[1] // HD
    here = lax.axis_index("exp")
    ids_all = lax.all_gather(expert_ids, "exp", axis=0, tiled=True)
    pos = lax.dynamic_slice_in_dim(positions(seg), here * rows, rows)
    normed = rms_scale(tokens, norm_attn)
    query = jnp.dot(normed, w_query, preferred_element_type=jnp.float32).reshape(
        rows, 2 * groups, HD
    )
    query = rotate(query, pos).astype(jnp.bfloat16).reshape(rows, groups, 2 * HD)
    keys = jnp.dot(normed, w_key, preferred_element_type=jnp.float32).reshape(rows, groups, HD)
    keys = rotate(keys, pos).astype(jnp.bfloat16)
    values = (
        jnp.dot(normed, w_value, preferred_element_type=jnp.float32)
        .astype(jnp.bfloat16)
        .reshape(rows, groups, HD)
    )
    keyval = jnp.concatenate([keys, values], axis=-1)
    query_heads, keyval_heads = (
        lax.all_to_all(query, "exp", split_axis=1, concat_axis=0, tiled=True),
        lax.all_to_all(keyval, "exp", split_axis=1, concat_axis=0, tiled=True),
    )
    kv_cache = jnp.zeros_like(keyval_heads).at[page_order[0]].set(keyval_heads)
    heads_out = attend(query_heads, keyval_heads, seg)
    attention = lax.psum_scatter(
        jnp.dot(heads_out, w_out, preferred_element_type=jnp.float32),
        "exp",
        scatter_dimension=0,
        tiled=True,
    )
    resid = tokens.astype(jnp.float32) + attention
    normed2 = rms_scale(resid, norm_moe)
    rows_all = lax.all_gather(normed2, "exp", axis=0, tiled=True)
    partial = expert_mix(rows_all, ids_all, w_router, w_gate, w_up, w_down)
    moe = lax.psum_scatter(partial, "exp", scatter_dimension=0, tiled=True)
    mixed = (resid + moe).astype(jnp.bfloat16)
    return (mixed, kv_cache)


def solution(mesh):
    placed = (
        P(("req", "exp"), None),
        P(),
        P(),
        P(),
        P(),
        P("exp", None),
        P(),
        P(),
        P("exp", None, None),
        P("exp", None, None),
        P("exp", None, None),
        P("req", None),
        P("req", None),
        P(("req", "exp"), None),
    )
    return jax.shard_map(
        shards,
        mesh=mesh,
        in_specs=placed,
        out_specs=(P(("req", "exp"), None), P("req", "exp", None)),
        check_vma=False,
    )
```

profile of v0, /device:TPU:0, one launch (start us, length us, event | category | flops | bytes accessed | tf_op | source)
XLA Modules:
  0.0 250.5 jit_solution(3685987123882004109)
XLA Ops:
  10.6 1.7 convolution_convert_fusion.1
  12.4 1.9 fusion.49
  15.4 6.3 %all-to-all-start = ((bf16[128,8,128]{0,2,1:T(8,128)(2,1)}), bf16[128,8,128]{0,2,1:T(8,128)(2,1)S(1)}, u32[]{:S(2)}, u32[]{:S(2)}) async-start(bf16[128,8,128]{0,2,1:T(8,128)(2,1)} %pad_maximum_fusion), calls=%async_computation | async-start | bytes 524288 | tf_op jit(solution)/shard_map/all_to_all | solution.py:133
  23.5 7.1 %all-to-all-done = bf16[128,8,128]{0,2,1:T(8,128)(2,1)S(1)} async-done(((bf16[128,8,128]{0,2,1:T(8,128)(2,1)}), bf16[128,8,128]{0,2,1:T(8,128)(2,1)S(1)}, u32[]{:S(2)}, u32[]{:S(2)}) %all-to-all-start) | async-done | bytes 262176 | tf_op jit(solution)/shard_map/all_to_all | solution.py:133
  30.6 3.4 %all-to-all-start.1 = ((bf16[128,8,128]{0,2,1:T(8,128)(2,1)}), bf16[128,8,128]{0,2,1:T(8,128)(2,1)S(1)}, u32[]{:S(2)}, u32[]{:S(2)}) async-start(bf16[128,8,128]{0,2,1:T(8,128)(2,1)} %bitcast.12), calls=%async_computation.1 | async-start | bytes 524288 | tf_op jit(solution)/shard_map/all_to_all | solution.py:132
  34.6 6.4 %all-to-all-done.1 = bf16[128,8,128]{0,2,1:T(8,128)(2,1)S(1)} async-done(((bf16[128,8,128]{0,2,1:T(8,128)(2,1)}), bf16[128,8,128]{0,2,1:T(8,128)(2,1)S(1)}, u32[]{:S(2)}, u32[]{:S(2)}) %all-to-all-start.1) | async-done | bytes 262176 | tf_op jit(solution)/shard_map/all_to_all | solution.py:132
  41.3 3.6 %fusion.51 = (f32[2,2,512]{2,1,0:T(2,128)S(1)}, f32[2,2,512,512]{2,3,1,0:T(8,128)}) fusion(pred[512,512]{0,1:T(8,128)(4,1)S(1)} %fusion.30, bf16[512,2,2,64]{0,3,2,1:T(8,128)(2,1)S(1)} %squeeze.14, bf16[512,2,128]{0,2,1:T(8,128)(2,1)S(1)} %reshape.234), kind=kOutput, calls=%fused_computation.90 | convolution fusion | flops 138412544 | bytes 4857856 | tf_op jit(solution)/shard_map/while/body/eval_jaxpr/sub | solution.py:54
  44.9 2.7 %fusion.28 = bf16[2,64,2,512]{3,1,2,0:T(8,128)(2,1)S(1)} fusion(f32[2,2,512,512]{2,3,1,0:T(8,128)} %get-tuple-element.33, f32[2,2,512]{2,1,0:T(2,128)S(1)} %get-tuple-element.32, bf16[512,2,128]{0,2,1:T(8,128)(2,1)S(1)} %reshape.234), kind=kOutput, calls=%fused_computation.33 | convolution fusion | flops 136445952 | bytes 4595712 | tf_op jit(solution)/shard_map/while/body/eval_jaxpr/kgqt,tkd->qkgd/dot_general | solution.py:56
  47.7 1.8 fusion.52
  49.6 43.3 %reduce-scatter.3.cloned.1.call-done = f32[128,1024]{1,0:T(8,128)} async-done(((f32[512,1024]{1,0:T(8,128)}), f32[128,1024]{1,0:T(8,128)}) %reduce-scatter.3.cloned.1.call-update) | async-done | bytes 524304 | tf_op jit(solution)/shard_map/reduce_scatter | solution.py:137
  94.1 1.9 multiply_convert_fusion.1
  96.1 13.3 %all_gather.6 = s32[512,8]{0,1:T(8,128)S(1)} all-gather(s32[128,8]{0,1:T(8,128)S(1)} %copy-done.11), channel_id=1, replica_groups=mesh['req'=8,'exp'=4] {'exp'}, dimensions={0}, use_global_device_ids=true | all-gather | bytes 20480 | tf_op jit(solution)/shard_map/all_gather | solution.py:116
  110.6 12.8 %all-gather.2.cloned.1.call-done = bf16[512,1024]{1,0:T(8,128)(2,1)} async-done(((bf16[128,1024]{1,0:T(8,128)(2,1)}), bf16[512,1024]{1,0:T(8,128)(2,1)}) %all-gather.2.cloned.1.call-update) | async-done | bytes 1048592 | tf_op jit(solution)/shard_map/all_gather | solution.py:145
  123.4 1.6 fusion.53
  125.1 33.2 %gather_fusion = f32[4096]{0:T(1024)S(1)} fusion(f32[512,32]{0,1:T(8,128)S(1)} %fusion.53, s32[4096]{0:T(1024)S(1)} %reshape.224), kind=kCustom, calls=%fused_computation | custom fusion | bytes 65536 | tf_op jit(solution)/shard_map/jit(take_along_axis)/gather | solution.py:69
  160.3 4.7 %fusion.6 = bf16[8,256,1024]{2,1,0:T(8,128)(2,1)S(1)} fusion(s32[8,512]{1,0:T(8,128)} %convolution_convert_fusion.2, pred[8,512]{1,0:T(8,128)(4,1)S(1)} %bitcast.100, bf16[512,1024]{1,0:T(8,128)(2,1)S(1)} %copy-done.5), kind=kOutput, calls=%fused_computation.15 | convolution fusion | flops 2151677952 | bytes 5263360 | tf_op jit(solution)/shard_map/est,td->esd/dot_general | solution.py:80
  165.1 2.0 copy-done.2
  167.0 7.7 %fusion.54 = f32[8,256,512]{2,1,0:T(8,128)} fusion(bf16[8,256,1024]{2,1,0:T(8,128)(2,1)S(1)} %fusion.6, bf16[8,1024,512]{2,1,0:T(8,128)(2,1)} %param.22), kind=kOutput, calls=%fused_computation.93 | convolution fusion | flops 2147483648 | bytes 16777216 | tf_op jit(solution)/shard_map/esd,edf->esf/dot_general | solution.py:83
  174.7 14.6 %convolution_convert_fusion = bf16[8,256,1024]{2,1,0:T(8,128)(2,1)} fusion(bf16[8,512,1024]{2,1,0:T(8,128)(2,1)} %param.24, f32[8,256,512]{2,1,0:T(8,128)} %fusion.54, bf16[8,256,1024]{2,1,0:T(8,128)(2,1)} %copy-done.2, bf16[8,1024,512]{2,1,0:T(8,128)(2,1)} %param.23), kind=kOutput, calls=%fused_computation.14 | convolution fusion | flops 4303355904 | bytes 29360128 | tf_op jit(solution)/shard_map/esf,efd->esd/dot_general | solution.py:86
  189.3 5.3 %fusion.9 = f32[512,1024,1]{1,0,2:T(8,128)S(1)} fusion(bf16[8,256,1024]{2,1,0:T(8,128)(2,1)} %convolution_convert_fusion, f32[8,512]{1,0:T(8,128)S(1)} %bitcast.97, s32[8,512]{1,0:T(8,128)S(1)} %copy-done.14, pred[8,512]{1,0:T(8,128)(4,1)S(1)} %bitcast.101), kind=kOutput, calls=%fused_computation.16 | convolution fusion | flops 2150629376 | bytes 6328320 | tf_op jit(solution)/shard_map/est,esd->td/dot_general | solution.py:91
  194.7 4.2 %bitcast_add_fusion = f32[512,1024]{1,0:T(8,128)} fusion(f32[512,1024,1]{1,0,2:T(8,128)S(1)} %fusion.9, bf16[8,256,1024]{2,1,0:T(8,128)(2,1)S(1)} %copy-done.15, f32[8,512]{1,0:T(8,128)S(1)} %bitcast.98, s32[8,512]{1,0:T(8,128)S(1)} %copy-done.14, pred[8,512]{1,0:T(8,128)(4,1)S(1)} %bitcast.102), kind=kOutput, calls=%fused_computation.18 | convolution fusion | flops 2155347968 | bytes 8425472 | tf_op jit(solution)/shard_map/est,esd->td/dot_general | solution.py:92
  199.3 14.2 %scatter_fusion = bf16[512,2,128]{2,1,0:T(2,128)(2,1)S(1)} fusion(bf16[512,2,128]{2,1,0:T(2,128)(2,1)S(1)} %broadcast_in_dim.101, s32[512]{0:T(512)S(1)} %bitcast.99, bf16[512,2,128]{2,1,0:T(2,128)(2,1)S(1)} %copy.53), kind=kCustom, calls=%fused_computation.1 | custom fusion | bytes 788480 | tf_op jit(solution)/shard_map/scatter | solution.py:135
  213.5 28.6 %reduce-scatter.5.cloned.1.call-done = f32[128,1024]{1,0:T(8,128)} async-done(((f32[512,1024]{1,0:T(8,128)}), f32[128,1024]{1,0:T(8,128)}) %reduce-scatter.5.cloned.1.call-update) | async-done | bytes 524304 | tf_op jit(solution)/shard_map/reduce_scatter | solution.py:147
  242.1 1.8 add_convert_fusion
  (79 shorter events, 12.1 us)
Async XLA Ops:
  7.2 14.6 %copy-start = (bf16[1024,1024]{1,0:T(8,128)(2,1)S(1)}, bf16[1024,1024]{1,0:T(8,128)(2,1)}, u32[]{:S(2)}) copy-start(bf16[1024,1024]{1,0:T(8,128)(2,1)} %param.16) | copy-start | bytes 6291460
  7.2 14.5 %copy-start.1 = (bf16[128,1024]{1,0:T(8,128)(2,1)S(1)}, bf16[128,1024]{1,0:T(8,128)(2,1)}, u32[]{:S(2)}) copy-start(bf16[128,1024]{1,0:T(8,128)(2,1)} %param.14) | copy-start | bytes 786436
  12.3 21.8 %copy-start.10 = (s32[1,512]{1,0:T(1,128)S(1)}, s32[1,512]{1,0:T(1,128)}, u32[]{:S(2)}) copy-start(s32[1,512]{1,0:T(1,128)} %param.25) | copy-start | bytes 6148
  15.4 15.2 %all-to-all-start = ((bf16[128,8,128]{0,2,1:T(8,128)(2,1)}), bf16[128,8,128]{0,2,1:T(8,128)(2,1)S(1)}, u32[]{:S(2)}, u32[]{:S(2)}) async-start(bf16[128,8,128]{0,2,1:T(8,128)(2,1)} %pad_maximum_fusion), calls=%async_computation | async-start | bytes 524288 | tf_op jit(solution)/shard_map/all_to_all | solution.py:133
  30.6 10.4 %all-to-all-start.1 = ((bf16[128,8,128]{0,2,1:T(8,128)(2,1)}), bf16[128,8,128]{0,2,1:T(8,128)(2,1)S(1)}, u32[]{:S(2)}, u32[]{:S(2)}) async-start(bf16[128,8,128]{0,2,1:T(8,128)(2,1)} %bitcast.12), calls=%async_computation.1 | async-start | bytes 524288 | tf_op jit(solution)/shard_map/all_to_all | solution.py:132
  34.0 58.9 %reduce-scatter.3.cloned.1.call-start = ((), (), s32[]{:S(2)}) async-start(), calls=%async_computation.4 | async-start | bytes 2621440 | tf_op jit(solution)/shard_map/reduce_scatter | solution.py:137
  34.6 10.3 %copy-start.6 = (bf16[512,2,128]{0,2,1:T(8,128)(2,1)}, bf16[512,2,128]{0,2,1:T(8,128)(2,1)S(1)}, u32[]{:S(2)}) copy-start(bf16[512,2,128]{0,2,1:T(8,128)(2,1)S(1)} %reshape.234) | copy-start | bytes 786436
  44.9 2.8 %copy-start.8 = (bf16[256,1024]{1,0:T(8,128)(2,1)S(1)}, bf16[256,1024]{1,0:T(8,128)(2,1)}, u32[]{:S(2)}) copy-start(bf16[256,1024]{1,0:T(8,128)(2,1)} %param.19) | copy-start | bytes 1572868
  47.7 1.9 copy-start.12
  47.7 48.4 %copy-start.11 = (s32[128,8]{0,1:T(8,128)S(1)}, s32[128,8]{0,1:T(8,128)}, u32[]{:S(2)}) copy-start(s32[128,8]{0,1:T(8,128)} %param.27) | copy-start | bytes 12292
  47.7 75.7 %copy-start.9 = (bf16[1024,32]{0,1:T(8,128)(2,1)S(1)}, bf16[1024,32]{0,1:T(8,128)(2,1)}, u32[]{:S(2)}) copy-start(bf16[1024,32]{0,1:T(8,128)(2,1)} %param.21) | copy-start | bytes 196612
  49.5 73.9 %all-gather.2.cloned.1.call-start = ((), (), s32[]{:S(2)}) async-start(), calls=%async_computation.5 | async-start | bytes 1310720 | tf_op jit(solution)/shard_map/all_gather | solution.py:145
  96.0 146.1 %reduce-scatter.5.cloned.1.call-start = ((), (), s32[]{:S(2)}) async-start(), calls=%async_computation.6 | async-start | bytes 2621440 | tf_op jit(solution)/shard_map/reduce_scatter | solution.py:147
  125.0 35.3 %copy-start.5 = (bf16[512,1024]{1,0:T(8,128)(2,1)S(1)}, bf16[512,1024]{1,0:T(8,128)(2,1)}, u32[]{:S(2)}) copy-start(bf16[512,1024]{1,0:T(8,128)(2,1)} %all-gather.2.cloned.1.call-done) | copy-start | bytes 3145732
  165.0 2.0 copy-start.2
  174.7 14.6 %copy-start.14 = (s32[8,512]{1,0:T(8,128)S(1)}, s32[8,512]{1,0:T(8,128)}, u32[]{:S(2)}) copy-start(s32[8,512]{1,0:T(8,128)} %convolution_convert_fusion.2) | copy-start | bytes 49156
  189.3 5.3 %copy-start.15 = (bf16[8,256,1024]{2,1,0:T(8,128)(2,1)S(1)}, bf16[8,256,1024]{2,1,0:T(8,128)(2,1)}, u32[]{:S(2)}) copy-start(bf16[8,256,1024]{2,1,0:T(8,128)(2,1)} %convolution_convert_fusion) | copy-start | bytes 12582916
  194.6 4.3 %copy-start.13 = (s32[1,512]{1,0:T(1,128)S(1)}, s32[1,512]{1,0:T(1,128)}, u32[]{:S(2)}) copy-start(s32[1,512]{1,0:T(1,128)} %param.26) | copy-start | bytes 6148
  194.6 4.3 %copy-start.7 = (bf16[512,2,128]{0,2,1:T(8,128)(2,1)S(1)}, bf16[512,2,128]{0,2,1:T(8,128)(2,1)}, u32[]{:S(2)}) copy-start(bf16[512,2,128]{0,2,1:T(8,128)(2,1)} %copy-done.6) | copy-start | bytes 786436
  194.6 47.4 %copy-start.3 = (f32[128,1024]{1,0:T(8,128)S(1)}, f32[128,1024]{1,0:T(8,128)}, u32[]{:S(2)}) copy-start(f32[128,1024]{1,0:T(8,128)} %reduce-scatter.3.cloned.1.call-done) | copy-start | bytes 1572868
  213.5 30.5 %copy-start.4 = (bf16[512,2,128]{2,1,0:T(2,128)(2,1)}, bf16[512,2,128]{2,1,0:T(2,128)(2,1)S(1)}, u32[]{:S(2)}) copy-start(bf16[512,2,128]{2,1,0:T(2,128)(2,1)S(1)} %scatter_fusion) | copy-start | bytes 786436
Sparse Core Ops, SparseCore 0:
  49.7 43.2 reduce-scatter.2
  96.1 27.2 all-gather.1
  199.0 43.0 reduce-scatter.4
where the time goes:
time: 251 us; the launch traced here: 250 us
  waiting for transfers between devices  98.3 us (39%)
  local copies, waits for them, and re-layouts  52.9 us (21%)
  matrix products  51.7 us (21%)
  between operations  14.1 us (6%)
  blocking collectives  13.3 us (5%)
  other arithmetic  10.3 us (4%)
  starting transfers between devices  9.88 us (4%)
    reduce_scatter x1, waiting for transfers between devices, shards(): lax.psum_scatter(jnp.dot(heads_out, w_out, preferred_element_type=jnp.flo...  43.3 us
    gather x5, local copies, waits for them, and re-layouts, expert_mix(): jnp.take_along_axis(logits, ids_all, axis=1)  35.4 us
    reduce_scatter x1, waiting for transfers between devices, shards(): moe = lax.psum_scatter(partial, 'exp', scatter_dimension=0, tiled=True)  28.6 us
    dot_general x1, matrix products, expert_mix(): jnp.einsum('esf,efd->esd', hidden, w_down, preferred_element_type=jnp.flo...  14.6 us
    scatter x1, local copies, waits for them, and re-layouts, shards(): kv_cache = jnp.zeros_like(keyval_heads).at[page_order[0]].set(keyval_heads)  14.2 us
    all_gather x1, blocking collectives, shards(): ids_all = lax.all_gather(expert_ids, 'exp', axis=0, tiled=True)  13.3 us
    all_gather x1, waiting for transfers between devices, shards(): rows_all = lax.all_gather(normed2, 'exp', axis=0, tiled=True)  12.8 us
    dot_general x1, matrix products, expert_mix(): jnp.einsum('esd,edf->esf', received, w_gate, preferred_element_type=jnp.f...  7.68 us
  transfers between devices with their start and end apart: 5, of which 5 were waited for; matrix products, arithmetic and copies ran while one was open for 7% of the time, Pallas kernels for 0%

commit v1 on v0

--- a/solution.py
+++ b/solution.py
@@ -5,6 +5,29 @@
 
 HD = 64
 CAP = 64
+
+
+def split_up(value, dim, size):
+    shape = value.shape
+    blocks = value.reshape(*shape[:dim], size, shape[dim] // size, *shape[dim + 1 :])
+    return jnp.moveaxis(blocks, dim, 0)
+
+
+def in_order(tiles, dim):
+    shape = list(tiles.shape[1:])
+    shape[dim] *= tiles.shape[0]
+    return jnp.moveaxis(tiles, 0, dim).reshape(shape)
+
+
+def exchange_in_pairs(x, axis, split_dim, concat_dim):
+    count, index = (lax.axis_size(axis), lax.axis_index(axis))
+    blocks = split_up(x, split_dim, count)
+    done = [blocks[index]]
+    for step in range(1, count):
+        sent = blocks[index ^ step]
+        done.append(lax.ppermute(sent, axis, [(i, i ^ step) for i in range(count)]))
+    blocks = jnp.stack(done)[index ^ jnp.arange(count)]
+    return in_order(blocks, concat_dim)
 
 
 def rms_scale(rows, gain):
@@ -129,7 +152,7 @@
     )
     keyval = jnp.concatenate([keys, values], axis=-1)
     query_heads, keyval_heads = (
-        lax.all_to_all(query, "exp", split_axis=1, concat_axis=0, tiled=True),
+        exchange_in_pairs(query, "exp", 1, 0),
         lax.all_to_all(keyval, "exp", split_axis=1, concat_axis=0, tiled=True),
     )
     kv_cache = jnp.zeros_like(keyval_heads).at[page_order[0]].set(keyval_heads)

time: 251 us -> 248 us (0.988)
  waiting for transfers between devices: 98.3 us -> 91.6 us
    ppermute x0 -> x3, waiting for transfers between devices: none -> 7.33 us  [exchange_in_pairs(): done.append(lax.ppermute(sent, axis, [(i, i ^ step) for i in range(count)]))]
    all_to_all x1, waiting for transfers between devices: 7.1 us -> 0.01 us  [shards(): lax.all_to_all(keyval, 'exp', split_axis=1, concat_axis=0, tiled=True)]
    all_to_all x1 -> x0, waiting for transfers between devices: 6.4 us -> none  [shards(): lax.all_to_all(query, 'exp', split_axis=1, concat_axis=0, tiled=True)]
    ppermute x0 -> x3, starting transfers between devices: none -> 4.6 us  [exchange_in_pairs(): done.append(lax.ppermute(sent, axis, [(i, i ^ step) for i in range(count)]))]
    all_to_all x1 -> x0, starting transfers between devices: 3.41 us -> none  [shards(): lax.all_to_all(query, 'exp', split_axis=1, concat_axis=0, tiled=True)]
  transfers between devices with their start and end apart: 5 -> 7, of which waited for: 5 -> 5; matrix products, arithmetic and copies ran while one was open for 7% -> 8% of each run, Pallas kernels for 0% -> 0%
where the time goes in v1:
time: 248 us; the launch traced here: 247 us
  waiting for transfers between devices  91.6 us (37%)
  local copies, waits for them, and re-layouts  54.7 us (22%)
  matrix products  52.7 us (21%)
  between operations  14.2 us (6%)
  blocking collectives  13.3 us (5%)
  starting transfers between devices  11 us (4%)
  other arithmetic  9.6 us (4%)
    reduce_scatter x1, waiting for transfers between devices, shards(): lax.psum_scatter(jnp.dot(heads_out, w_out, preferred_element_type=jnp.flo...  42.8 us
    gather x5, local copies, waits for them, and re-layouts, expert_mix(): jnp.take_along_axis(logits, ids_all, axis=1)  35.4 us
    reduce_scatter x1, waiting for transfers between devices, shards(): moe = lax.psum_scatter(partial, 'exp', scatter_dimension=0, tiled=True)  28.6 us
    dot_general x1, matrix products, expert_mix(): jnp.einsum('esf,efd->esd', hidden, w_down, preferred_element_type=jnp.flo...  14.6 us
    scatter x1, local copies, waits for them, and re-layouts, shards(): kv_cache = jnp.zeros_like(keyval_heads).at[page_order[0]].set(keyval_heads)  14.2 us
    all_gather x1, blocking collectives, shards(): ids_all = lax.all_gather(expert_ids, 'exp', axis=0, tiled=True)  13.3 us
    all_gather x1, waiting for transfers between devices, shards(): rows_all = lax.all_gather(normed2, 'exp', axis=0, tiled=True)  12.9 us
    dot_general x1, matrix products, expert_mix(): jnp.einsum('esd,edf->esf', received, w_gate, preferred_element_type=jnp.f...  7.68 us
  transfers between devices with their start and end apart: 7, of which 5 were waited for; matrix products, arithmetic and copies ran while one was open for 8% of the time, Pallas kernels for 0%

profile of v1, /device:TPU:0, one launch (start us, length us, event | category | flops | bytes accessed | tf_op | source)
XLA Modules:
  0.0 247.1 jit_solution(5535986728086567876)
XLA Ops:
  10.6 1.7 convolution_convert_fusion.1
  12.4 1.9 fusion.50
  15.4 6.4 %all-to-all-start = ((bf16[128,8,128]{0,2,1:T(8,128)(2,1)}), bf16[128,8,128]{0,2,1:T(8,128)(2,1)S(1)}, u32[]{:S(2)}, u32[]{:S(2)}) async-start(bf16[128,8,128]{0,2,1:T(8,128)(2,1)} %pad_maximum_fusion), calls=%async_computation | async-start | bytes 524288 | tf_op jit(solution)/shard_map/all_to_all | solution.py:156
  23.0 2.1 collective-permute-start
  25.2 2.4 collective-permute-start.1
  28.2 2.2 collective-permute-done
  30.4 5.1 %collective-permute-done.1 = bf16[128,2,128]{2,0,1:T(8,128)(2,1)S(1)} collective-permute-done((bf16[128,2,128]{2,0,1:T(8,128)(2,1)S(1)}, bf16[128,2,128]{2,0,1:T(8,128)(2,1)S(1)}, u32[]{:S(2)}, u32[]{:S(2)}) %collective-permute-start.1) | collective-permute-done | bytes 65568 | tf_op jit(solution)/shard_map/ppermute | solution.py:28
  37.5 4.6 %fusion.52 = (f32[2,2,512]{2,1,0:T(2,128)S(1)}, f32[2,2,512,512]{2,3,1,0:T(8,128)}) fusion(pred[512,512]{0,1:T(8,128)(4,1)S(1)} %fusion.30, bf16[512,2,2,64]{0,3,2,1:T(8,128)(2,1)} %squeeze.26, bf16[512,2,128]{0,2,1:T(8,128)(2,1)S(1)} %reshape.262), kind=kOutput, calls=%fused_computation.99 | convolution fusion | flops 138412544 | bytes 4857856 | tf_op jit(solution)/shard_map/while/body/eval_jaxpr/sub | solution.py:77
  42.2 2.7 %fusion.28 = bf16[2,64,2,512]{3,1,2,0:T(8,128)(2,1)S(1)} fusion(f32[2,2,512,512]{2,3,1,0:T(8,128)} %get-tuple-element.37, f32[2,2,512]{2,1,0:T(2,128)S(1)} %get-tuple-element.36, bf16[512,2,128]{0,2,1:T(8,128)(2,1)S(1)} %reshape.262), kind=kOutput, calls=%fused_computation.34 | convolution fusion | flops 136445952 | bytes 4595712 | tf_op jit(solution)/shard_map/while/body/eval_jaxpr/kgqt,tkd->qkgd/dot_general | solution.py:79
  44.9 1.8 fusion.53
  46.9 42.8 %reduce-scatter.3.cloned.1.call-done = f32[128,1024]{1,0:T(8,128)} async-done(((f32[512,1024]{1,0:T(8,128)}), f32[128,1024]{1,0:T(8,128)}) %reduce-scatter.3.cloned.1.call-update) | async-done | bytes 524304 | tf_op jit(solution)/shard_map/reduce_scatter | solution.py:160
  90.8 1.9 multiply_convert_fusion.1
  92.8 13.3 %all_gather.6 = s32[512,8]{0,1:T(8,128)S(1)} all-gather(s32[128,8]{0,1:T(8,128)S(1)} %copy-done.11), channel_id=1, replica_groups=mesh['req'=8,'exp'=4] {'exp'}, dimensions={0}, use_global_device_ids=true | all-gather | bytes 20480 | tf_op jit(solution)/shard_map/all_gather | solution.py:139
  107.2 12.9 %all-gather.2.cloned.1.call-done = bf16[512,1024]{1,0:T(8,128)(2,1)} async-done(((bf16[128,1024]{1,0:T(8,128)(2,1)}), bf16[512,1024]{1,0:T(8,128)(2,1)}) %all-gather.2.cloned.1.call-update) | async-done | bytes 1048592 | tf_op jit(solution)/shard_map/all_gather | solution.py:168
  121.7 33.2 %gather_fusion.1 = f32[4096]{0:T(1024)S(1)} fusion(f32[512,32]{0,1:T(8,128)S(1)} %fusion.54, s32[4096]{0:T(1024)S(1)} %reshape.252), kind=kCustom, calls=%fused_computation.1 | custom fusion | bytes 65536 | tf_op jit(solution)/shard_map/jit(take_along_axis)/gather | solution.py:92
  157.0 4.7 %fusion.6 = bf16[8,256,1024]{2,1,0:T(8,128)(2,1)S(1)} fusion(s32[8,512]{1,0:T(8,128)} %convolution_convert_fusion.2, pred[8,512]{1,0:T(8,128)(4,1)S(1)} %bitcast.113, bf16[512,1024]{1,0:T(8,128)(2,1)S(1)} %copy-done.5), kind=kOutput, calls=%fused_computation.16 | convolution fusion | flops 2151677952 | bytes 5263360 | tf_op jit(solution)/shard_map/est,td->esd/dot_general | solution.py:103
  161.7 2.0 copy-done.2
  163.7 7.7 %fusion.55 = f32[8,256,512]{2,1,0:T(8,128)} fusion(bf16[8,256,1024]{2,1,0:T(8,128)(2,1)S(1)} %fusion.6, bf16[8,1024,512]{2,1,0:T(8,128)(2,1)} %param.22), kind=kOutput, calls=%fused_computation.102 | convolution fusion | flops 2147483648 | bytes 16777216 | tf_op jit(solution)/shard_map/esd,edf->esf/dot_general | solution.py:106
  171.4 14.6 %convolution_convert_fusion = bf16[8,256,1024]{2,1,0:T(8,128)(2,1)} fusion(bf16[8,512,1024]{2,1,0:T(8,128)(2,1)} %param.24, f32[8,256,512]{2,1,0:T(8,128)} %fusion.55, bf16[8,256,1024]{2,1,0:T(8,128)(2,1)} %copy-done.2, bf16[8,1024,512]{2,1,0:T(8,128)(2,1)} %param.23), kind=kOutput, calls=%fused_computation.15 | convolution fusion | flops 4303355904 | bytes 29360128 | tf_op jit(solution)/shard_map/esf,efd->esd/dot_general | solution.py:109
  186.0 5.3 %fusion.9 = f32[512,1024,1]{1,0,2:T(8,128)S(1)} fusion(bf16[8,256,1024]{2,1,0:T(8,128)(2,1)} %convolution_convert_fusion, f32[8,512]{1,0:T(8,128)S(1)} %bitcast.110, s32[8,512]{1,0:T(8,128)S(1)} %copy-done.14, pred[8,512]{1,0:T(8,128)(4,1)S(1)} %bitcast.114), kind=kOutput, calls=%fused_computation.17 | convolution fusion | flops 2150629376 | bytes 6328320 | tf_op jit(solution)/shard_map/est,esd->td/dot_general | solution.py:114
  191.3 4.2 %bitcast_add_fusion = f32[512,1024]{1,0:T(8,128)} fusion(f32[512,1024,1]{1,0,2:T(8,128)S(1)} %fusion.9, bf16[8,256,1024]{2,1,0:T(8,128)(2,1)S(1)} %copy-done.15, f32[8,512]{1,0:T(8,128)S(1)} %bitcast.111, s32[8,512]{1,0:T(8,128)S(1)} %copy-done.14, pred[8,512]{1,0:T(8,128)(4,1)S(1)} %bitcast.115), kind=kOutput, calls=%fused_computation.19 | convolution fusion | flops 2155347968 | bytes 8425472 | tf_op jit(solution)/shard_map/est,esd->td/dot_general | solution.py:115
  196.0 14.2 %scatter_fusion = bf16[512,2,128]{2,1,0:T(2,128)(2,1)S(1)} fusion(bf16[512,2,128]{2,1,0:T(2,128)(2,1)S(1)} %broadcast_in_dim.102, s32[512]{0:T(512)S(1)} %bitcast.112, bf16[512,2,128]{2,1,0:T(2,128)(2,1)S(1)} %copy.74), kind=kCustom, calls=%fused_computation.2 | custom fusion | bytes 788480 | tf_op jit(solution)/shard_map/scatter | solution.py:158
  210.2 28.6 %reduce-scatter.5.cloned.1.call-done = f32[128,1024]{1,0:T(8,128)} async-done(((f32[512,1024]{1,0:T(8,128)}), f32[128,1024]{1,0:T(8,128)}) %reduce-scatter.5.cloned.1.call-update) | async-done | bytes 524304 | tf_op jit(solution)/shard_map/reduce_scatter | solution.py:170
  238.8 1.8 add_convert_fusion
  (92 shorter events, 14.9 us)
Async XLA Ops:
  7.2 14.6 %copy-start = (bf16[1024,1024]{1,0:T(8,128)(2,1)S(1)}, bf16[1024,1024]{1,0:T(8,128)(2,1)}, u32[]{:S(2)}) copy-start(bf16[1024,1024]{1,0:T(8,128)(2,1)} %param.16) | copy-start | bytes 6291460
  7.2 14.5 %copy-start.1 = (bf16[128,1024]{1,0:T(8,128)(2,1)S(1)}, bf16[128,1024]{1,0:T(8,128)(2,1)}, u32[]{:S(2)}) copy-start(bf16[128,1024]{1,0:T(8,128)(2,1)} %param.14) | copy-start | bytes 786436
  12.4 15.4 %copy-start.10 = (s32[1,512]{1,0:T(1,128)S(1)}, s32[1,512]{1,0:T(1,128)}, u32[]{:S(2)}) copy-start(s32[1,512]{1,0:T(1,128)} %param.25) | copy-start | bytes 6148
  15.4 21.8 %all-to-all-start = ((bf16[128,8,128]{0,2,1:T(8,128)(2,1)}), bf16[128,8,128]{0,2,1:T(8,128)(2,1)S(1)}, u32[]{:S(2)}, u32[]{:S(2)}) async-start(bf16[128,8,128]{0,2,1:T(8,128)(2,1)} %pad_maximum_fusion), calls=%async_computation | async-start | bytes 524288 | tf_op jit(solution)/shard_map/all_to_all | solution.py:156
  21.7 67.9 %reduce-scatter.3.cloned.1.call-start = ((), (), s32[]{:S(2)}) async-start(), calls=%async_computation.3 | async-start | bytes 2621440 | tf_op jit(solution)/shard_map/reduce_scatter | solution.py:160
  23.0 7.4 %collective-permute-start = (bf16[128,2,128]{2,0,1:T(8,128)(2,1)S(1)}, bf16[128,2,128]{2,0,1:T(8,128)(2,1)S(1)}, u32[]{:S(2)}, u32[]{:S(2)}) collective-permute-start(bf16[128,2,128]{2,0,1:T(8,128)(2,1)S(1)} %bitcast.103), channel_id=1, source_target_pairs={{0,1},{1,0},{2,3},{3,2},{4,5},{5,4},{6,7},{7,6},{8,9},{9,8},{10,11... | collective-permute-start | bytes 196616 | tf_op jit(solution)/shard_map/ppermute | solution.py:28
  25.2 10.3 %collective-permute-start.1 = (bf16[128,2,128]{2,0,1:T(8,128)(2,1)S(1)}, bf16[128,2,128]{2,0,1:T(8,128)(2,1)S(1)}, u32[]{:S(2)}, u32[]{:S(2)}) collective-permute-start(bf16[128,2,128]{2,0,1:T(8,128)(2,1)S(1)} %bitcast.104), channel_id=1, source_target_pairs={{0,2},{1,3},{2,0},{3,1},{4,6},{5,7},{6,4},{7,5},{8,10},{9,11},{10,... | collective-permute-start | bytes 196616 | tf_op jit(solution)/shard_map/ppermute | solution.py:28
  27.8 7.8 %collective-permute-start.2 = (bf16[128,2,128]{2,0,1:T(8,128)(2,1)S(1)}, bf16[128,2,128]{2,0,1:T(8,128)(2,1)S(1)}, u32[]{:S(2)}, u32[]{:S(2)}) collective-permute-start(bf16[128,2,128]{2,0,1:T(8,128)(2,1)S(1)} %bitcast.105), channel_id=1, source_target_pairs={{0,3},{1,2},{2,1},{3,0},{4,7},{5,6},{6,5},{7,4},{8,11},{9,10},{10,... | collective-permute-start | bytes 196616 | tf_op jit(solution)/shard_map/ppermute | solution.py:28
  37.5 7.4 %copy-start.6 = (bf16[512,2,128]{0,2,1:T(8,128)(2,1)}, bf16[512,2,128]{0,2,1:T(8,128)(2,1)S(1)}, u32[]{:S(2)}) copy-start(bf16[512,2,128]{0,2,1:T(8,128)(2,1)S(1)} %reshape.262) | copy-start | bytes 786436
  42.1 2.8 %copy-start.8 = (bf16[256,1024]{1,0:T(8,128)(2,1)S(1)}, bf16[256,1024]{1,0:T(8,128)(2,1)}, u32[]{:S(2)}) copy-start(bf16[256,1024]{1,0:T(8,128)(2,1)} %param.19) | copy-start | bytes 1572868
  44.9 1.9 copy-start.12
  44.9 47.8 %copy-start.11 = (s32[128,8]{0,1:T(8,128)S(1)}, s32[128,8]{0,1:T(8,128)}, u32[]{:S(2)}) copy-start(s32[128,8]{0,1:T(8,128)} %param.27) | copy-start | bytes 12292
  44.9 75.2 %copy-start.9 = (bf16[1024,32]{0,1:T(8,128)(2,1)S(1)}, bf16[1024,32]{0,1:T(8,128)(2,1)}, u32[]{:S(2)}) copy-start(bf16[1024,32]{0,1:T(8,128)(2,1)} %param.21) | copy-start | bytes 196612
  46.8 73.3 %all-gather.2.cloned.1.call-start = ((), (), s32[]{:S(2)}) async-start(), calls=%async_computation.4 | async-start | bytes 1310720 | tf_op jit(solution)/shard_map/all_gather | solution.py:168
  92.7 146.1 %reduce-scatter.5.cloned.1.call-start = ((), (), s32[]{:S(2)}) async-start(), calls=%async_computation.5 | async-start | bytes 2621440 | tf_op jit(solution)/shard_map/reduce_scatter | solution.py:170
  121.7 35.3 %copy-start.5 = (bf16[512,1024]{1,0:T(8,128)(2,1)S(1)}, bf16[512,1024]{1,0:T(8,128)(2,1)}, u32[]{:S(2)}) copy-start(bf16[512,1024]{1,0:T(8,128)(2,1)} %all-gather.2.cloned.1.call-done) | copy-start | bytes 3145732
  161.7 2.0 copy-start.2
  171.4 14.6 %copy-start.14 = (s32[8,512]{1,0:T(8,128)S(1)}, s32[8,512]{1,0:T(8,128)}, u32[]{:S(2)}) copy-start(s32[8,512]{1,0:T(8,128)} %convolution_convert_fusion.2) | copy-start | bytes 49156
  186.0 5.3 %copy-start.15 = (bf16[8,256,1024]{2,1,0:T(8,128)(2,1)S(1)}, bf16[8,256,1024]{2,1,0:T(8,128)(2,1)}, u32[]{:S(2)}) copy-start(bf16[8,256,1024]{2,1,0:T(8,128)(2,1)} %convolution_convert_fusion) | copy-start | bytes 12582916
  191.3 4.3 %copy-start.13 = (s32[1,512]{1,0:T(1,128)S(1)}, s32[1,512]{1,0:T(1,128)}, u32[]{:S(2)}) copy-start(s32[1,512]{1,0:T(1,128)} %param.26) | copy-start | bytes 6148
  191.3 4.3 %copy-start.7 = (bf16[512,2,128]{0,2,1:T(8,128)(2,1)S(1)}, bf16[512,2,128]{0,2,1:T(8,128)(2,1)}, u32[]{:S(2)}) copy-start(bf16[512,2,128]{0,2,1:T(8,128)(2,1)} %copy-done.6) | copy-start | bytes 786436
  191.3 47.4 %copy-start.3 = (f32[128,1024]{1,0:T(8,128)S(1)}, f32[128,1024]{1,0:T(8,128)}, u32[]{:S(2)}) copy-start(f32[128,1024]{1,0:T(8,128)} %reduce-scatter.3.cloned.1.call-done) | copy-start | bytes 1572868
  210.2 30.5 %copy-start.4 = (bf16[512,2,128]{2,1,0:T(2,128)(2,1)}, bf16[512,2,128]{2,1,0:T(2,128)(2,1)S(1)}, u32[]{:S(2)}) copy-start(bf16[512,2,128]{2,1,0:T(2,128)(2,1)S(1)} %scatter_fusion) | copy-start | bytes 786436
Sparse Core Ops, SparseCore 0:
  46.9 42.6 reduce-scatter.2
  92.8 27.2 all-gather.1
  195.7 43.0 reduce-scatter.4
